TPU v7x, 256 devices: a whole 4x4x8 slice. The times are simulated.
256 devices in a mesh: seq: 64 (over y, z, core), ch: 4 (over x).
Axes of the slice: x: 4, y: 4, z: 8, core: 2. Of those that a mesh axis runs over, the one named last changes fastest.
Arguments:
- query_stream: bfloat16 [16384, 4096], P('seq', 'ch'), may hold values from -16 to 16
- key_stream: bfloat16 [16384, 4096], P('seq', 'ch'), may hold values from -6 to 6
- value_stream: bfloat16 [16384, 4096], P('seq', 'ch'), may hold values from -6 to 6
- filter_taps: float32 [4096, 128], P('ch'), may hold values from -0.5 to 0.5
- out_weight: bfloat16 [4096, 4096], P('seq', 'ch'), may hold values from -0.09375 to 0.09375
- upstream: bfloat16 [16384, 4096], P('seq', 'ch'), may hold values from -6 to 6
Outputs:
- mixed: bfloat16 [16384, 4096], P('seq', 'ch')
- grad_query: bfloat16 [16384, 4096], P('seq', 'ch')
- grad_key: bfloat16 [16384, 4096], P('seq', 'ch')
- grad_value: bfloat16 [16384, 4096], P('seq', 'ch')
- grad_filter: float32 [4096, 128], P('ch')
- grad_weight: float32 [4096, 4096], P('seq', 'ch')
All inputs are finite; a program needn't handle non-finite values.
Results may differ from a plain program's by a relative error of at most 0.0057.
Values may be sent and summed in bfloat16 or wider, within the bound.
No kernel may reach another device: no remote copies, remote signals or barrier semaphores. Data moves between devices by JAX's collectives and lax.ppermute only.
A program may use at most 128 MiB of HBM per device.

v0:
```python
import jax
import jax.numpy as jnp
from jax import lax
from jax.sharding import PartitionSpec as P


def from_behind(value, axis, steps):
    count = lax.axis_size(axis)
    initial, last = (max(0, -steps), min(count, count - steps))
    return lax.ppermute(value, axis, [(source, source + steps) for source in range(initial, last)])


def depthwise(signal, kernel):
    output = lax.conv_general_dilated(
        signal[None],
        kernel[:, None, :],
        (1,),
        "VALID",
        dimension_numbers=("NWC", "WIO", "NWC"),
        feature_group_count=signal.shape[1],
        precision=lax.Precision.HIGHEST,
    )
    return output[0]


def body(query_stream, key_stream, value_stream, filter_taps, out_weight, upstream):
    rows_here = query_stream.shape[0]
    tap_count = filter_taps.shape[1]
    keyed = (key_stream.astype(jnp.float32) * value_stream.astype(jnp.float32)).astype(jnp.bfloat16)
    rim_before = from_behind(keyed[rows_here - (tap_count - 1) :], "seq", 1)
    front_pad = jnp.concatenate([rim_before, keyed], axis=0).astype(jnp.float32)
    response = depthwise(front_pad, filter_taps.T[::-1])
    query_wide = query_stream.astype(jnp.float32)
    gated = (query_wide * response).astype(jnp.bfloat16)
    gated_full = lax.all_gather(gated, "ch", axis=1, tiled=True)
    weight_cols = lax.all_gather(out_weight, "seq", axis=0, tiled=True)
    mixed = jnp.dot(gated_full, weight_cols, preferred_element_type=jnp.float32).astype(
        jnp.bfloat16
    )
    partial_terms = lax.dot_general(
        upstream, weight_cols, (((1,), (1,)), ((), ())), preferred_element_type=jnp.float32
    )
    grad_gated = lax.psum_scatter(partial_terms, "ch", scatter_dimension=1, tiled=True)
    grad_query = (grad_gated * response).astype(jnp.bfloat16)
    grad_response = grad_gated * query_wide
    rim_after = from_behind(grad_response[: tap_count - 1], "seq", -1)
    back_pad = jnp.concatenate([grad_response, rim_after], axis=0)
    grad_keyed = depthwise(back_pad, filter_taps.T)
    grad_key = (grad_keyed * value_stream.astype(jnp.float32)).astype(jnp.bfloat16)
    grad_value = (grad_keyed * key_stream.astype(jnp.float32)).astype(jnp.bfloat16)
    filter_local = depthwise(front_pad, grad_response)[::-1].T
    grad_filter = lax.psum(filter_local, "seq")
    columns = lax.slice_in_dim(gated_full, 0, lax.axis_size("seq") * out_weight.shape[0], axis=1)
    grad_weight = lax.psum_scatter(
        lax.dot_general(
            columns, upstream, (((0,), (0,)), ((), ())), preferred_element_type=jnp.float32
        ),
        "seq",
        scatter_dimension=0,
        tiled=True,
    )
    return (mixed, grad_query, grad_key, grad_value, grad_filter, grad_weight)


def solution(mesh):
    in_specs = (
        P("seq", "ch"),
        P("seq", "ch"),
        P("seq", "ch"),
        P("ch", None),
        P("seq", "ch"),
        P("seq", "ch"),
    )
    out_specs = (
        P("seq", "ch"),
        P("seq", "ch"),
        P("seq", "ch"),
        P("seq", "ch"),
        P("ch", None),
        P("seq", "ch"),
    )
    return jax.shard_map(body, mesh=mesh, in_specs=in_specs, out_specs=out_specs, check_vma=False)
```

profile of v0, /device:TPU:2, one launch (start us, length us, event | category | flops | bytes accessed | tf_op | source)
XLA Modules:
  0.0 614.4 jit_solution(9339220841736007042)
XLA Ops:
  7.2 0.0 all-gather.5.cloned.1.call-start
  7.2 0.7 all-gather.5.cloned.1.call-update
  7.9 0.0 reduce-scatter.3.cloned.1.call-start
  8.0 88.8 %all-gather.5.cloned.1.call-done = bf16[4096,1024]{1,0:T(8,128)(2,1)} async-done(((bf16[64,1024]{1,0:T(8,128)(2,1)}), bf16[4096,1024]{1,0:T(8,128)(2,1)}) %all-gather.5.cloned.1.call-update) | async-done | bytes 8388624 | tf_op jit(solution)/shard_map/all_gather | solution.py:36
  96.8 7.7 %fusion.12 = f32[256,4096]{1,0:T(8,128)} fusion(bf16[256,1024]{1,0:T(8,128)(2,1)S(1)} %copy-done, bf16[4096,1024]{1,0:T(8,128)(2,1)} %all-gather.5.cloned.1.call-done), kind=kOutput, calls=%fused_computation.22 | convolution fusion | flops 2147483648 | bytes 13107200 | tf_op jit(solution)/shard_map/dot_general | solution.py:40
  104.5 0.0 all-gather.3.cloned.1.call-start
  104.5 45.0 %reduce-scatter.3.cloned.1.call-done = f32[256,1024]{1,0:T(8,128)} async-done(((f32[256,4096]{1,0:T(8,128)}), f32[256,1024]{1,0:T(8,128)}) %reduce-scatter.3.cloned.1.call-update) | async-done | bytes 1048592 | tf_op jit(solution)/shard_map/reduce_scatter | solution.py:43
  149.5 1.4 convert_multiply_fusion.3
  151.0 1.3 collective-permute-start.1
  152.3 0.4 copy.20
  152.7 2.2 collective-permute-done.1
  154.9 1.2 maximum_bitcast_fusion
  156.1 10.6 %fusion = f32[1,256,1024]{2,0,1:T(1,128)S(1)} fusion(f32[128,1,1024]{2,1,0:T(1,128)S(1)} %copy.20, f32[1,383,1024]{2,1,0:T(8,128)S(1)} %maximum_bitcast_fusion), kind=kOutput, calls=%fused_computation.1 | convolution fusion | flops 402653184 | bytes 3141632 | tf_op jit(solution)/shard_map/conv_general_dilated | solution.py:14
  166.7 1.5 fusion.7
  168.2 0.1 slice.8
  168.3 8.5 %collective-permute-start = (bf16[127,1024]{1,0:T(8,128)(2,1)S(1)}, bf16[127,1024]{1,0:T(8,128)(2,1)S(1)}, u32[]{:S(2)}, u32[]{:S(2)}) collective-permute-start(bf16[127,1024]{1,0:T(8,128)(2,1)S(1)} %slice.8), channel_id=1, source_target_pairs={{0,4},{4,8},{8,12},{12,16},{16,20},{20,24},{24,28},{28,32},{32,36}... | collective-permute-start | bytes 780296 | tf_op jit(solution)/shard_map/ppermute | solution.py:10
  176.8 0.7 rev.6
  177.6 0.4 copy.18
  178.0 0.1 maximum_bitcast_fusion.1
  178.2 10.6 %fusion.4 = f32[1,256,1024]{2,0,1:T(1,128)S(1)} fusion(f32[128,1,1024]{2,1,0:T(1,128)S(1)} %copy.18, bf16[1,383,1024]{2,1,0:T(8,128)(2,1)S(1)} %maximum_bitcast_fusion.1), kind=kOutput, calls=%fused_computation.11 | convolution fusion | flops 402653184 | bytes 2357248 | tf_op jit(solution)/shard_map/conv_general_dilated | solution.py:14
  188.8 1.4 fusion.10
  190.2 0.0 all-reduce.2.cloned.1.call-start
  190.3 10.7 %fusion.2 = f32[1,128,1024]{2,0,1:T(1,128)S(1)} fusion(bf16[1,383,1024]{2,1,0:T(8,128)(2,1)S(1)} %maximum_bitcast_fusion.1, f32[256,1,1024]{2,0,1:T(8,128)S(1)} %bitcast.29), kind=kOutput, calls=%fused_computation.9 | convolution fusion | flops 402653184 | bytes 2357248 | tf_op jit(solution)/shard_map/conv_general_dilated | solution.py:14
  201.0 0.1 copy.40
  201.1 2.6 rev.7
  203.7 0.2 reduce-scatter.5.cloned.1.call-start
  203.9 23.9 %all-gather.3.cloned.1.call-done = bf16[256,4096]{1,0:T(8,128)(2,1)} async-done(((bf16[256,1024]{1,0:T(8,128)(2,1)}), bf16[256,4096]{1,0:T(8,128)(2,1)}) %all-gather.3.cloned.1.call-update) | async-done | bytes 2097168 | tf_op jit(solution)/shard_map/all_gather | solution.py:35
  227.9 9.7 %fusion.13 = f32[4096,1024]{1,0:T(8,128)} fusion(bf16[256,4096]{1,0:T(8,128)(2,1)} %all-gather.3.cloned.1.call-done, bf16[256,1024]{1,0:T(8,128)(2,1)S(1)} %copy-done), kind=kOutput, calls=%fused_computation.23 | convolution fusion | flops 2147483648 | bytes 19398656 | tf_op jit(solution)/shard_map/dot_general | solution.py:55
  237.6 178.5 %all-reduce.2.cloned.1.call-done = f32[1024,128]{0,1:T(8,128)} async-done(((f32[1024,128]{0,1:T(8,128)}), f32[1024,128]{0,1:T(8,128)}) %all-reduce.2.cloned.1.call-update) | async-done | bytes 524304 | tf_op jit(solution)/shard_map/psum | solution.py:52
  416.1 2.0 copy.23
  418.1 6.5 %convolution_convert_fusion = bf16[256,1024]{1,0:T(8,128)(2,1)} fusion(bf16[256,4096]{1,0:T(8,128)(2,1)S(1)} %copy-done.4, bf16[4096,1024]{1,0:T(8,128)(2,1)} %all-gather.5.cloned.1.call-done), kind=kOutput, calls=%fused_computation.8 | convolution fusion | flops 2147745792 | bytes 11010048 | tf_op jit(solution)/shard_map/dot_general | solution.py:37
  424.6 183.2 %reduce-scatter.5.cloned.1.call-done = f32[64,1024]{1,0:T(8,128)} async-done(((f32[4096,1024]{1,0:T(8,128)}), f32[64,1024]{1,0:T(8,128)}) %reduce-scatter.5.cloned.1.call-update) | async-done | bytes 262160 | tf_op jit(solution)/shard_map/reduce_scatter | solution.py:54
  (28 shorter events, 0.2 us)
Async XLA Ops:
  7.2 89.6 %copy-start = (bf16[256,1024]{1,0:T(8,128)(2,1)S(1)}, bf16[256,1024]{1,0:T(8,128)(2,1)}, u32[]{:S(2)}) copy-start(bf16[256,1024]{1,0:T(8,128)(2,1)} %param.11) | copy-start | bytes 1572868
  7.2 89.6 %all-gather.5.cloned.1.call-start = ((), (), s32[]{:S(2)}) async-start(), calls=%async_computation.3 | async-start | bytes 8519680 | tf_op jit(solution)/shard_map/all_gather | solution.py:36
  7.9 141.6 %reduce-scatter.3.cloned.1.call-start = ((), (), s32[]{:S(2)}) async-start(), calls=%async_computation.4 | async-start | bytes 5242880 | tf_op jit(solution)/shard_map/reduce_scatter | solution.py:43
  104.4 45.1 %copy-start.5 = (bf16[256,1024]{1,0:T(8,128)(2,1)S(1)}, bf16[256,1024]{1,0:T(8,128)(2,1)}, u32[]{:S(2)}) copy-start(bf16[256,1024]{1,0:T(8,128)(2,1)} %param.6) | copy-start | bytes 1572868
  104.5 47.8 %copy-start.7 = (f32[1024,128]{1,0:T(8,128)S(1)}, f32[1024,128]{1,0:T(8,128)}, u32[]{:S(2)}) copy-start(f32[1024,128]{1,0:T(8,128)} %param.9) | copy-start | bytes 1572868
  104.5 123.4 %all-gather.3.cloned.1.call-start = ((), (), s32[]{:S(2)}) async-start(), calls=%async_computation.2 | async-start | bytes 2621440 | tf_op jit(solution)/shard_map/all_gather | solution.py:35
  150.9 5.2 copy-start.1
  151.0 3.9 collective-permute-start.1
  156.1 10.6 %copy-start.9 = (bf16[256,1024]{1,0:T(8,128)(2,1)S(1)}, bf16[256,1024]{1,0:T(8,128)(2,1)}, u32[]{:S(2)}) copy-start(bf16[256,1024]{1,0:T(8,128)(2,1)} %param.7) | copy-start | bytes 1572868
  156.1 10.6 %copy-start.10 = (bf16[256,1024]{1,0:T(8,128)(2,1)S(1)}, bf16[256,1024]{1,0:T(8,128)(2,1)}, u32[]{:S(2)}) copy-start(bf16[256,1024]{1,0:T(8,128)(2,1)} %param.8) | copy-start | bytes 1572868
  166.7 10.1 %copy-start.8 = (f32[1024,128]{1,0:T(8,128)S(1)}, f32[1024,128]{1,0:T(8,128)}, u32[]{:S(2)}) copy-start(f32[1024,128]{1,0:T(8,128)} %param.9) | copy-start | bytes 1572868
  168.3 9.7 %collective-permute-start = (bf16[127,1024]{1,0:T(8,128)(2,1)S(1)}, bf16[127,1024]{1,0:T(8,128)(2,1)S(1)}, u32[]{:S(2)}, u32[]{:S(2)}) collective-permute-start(bf16[127,1024]{1,0:T(8,128)(2,1)S(1)} %slice.8), channel_id=1, source_target_pairs={{0,4},{4,8},{8,12},{12,16},{16,20},{20,24},{24,28},{28,32},{32,36}... | collective-permute-start | bytes 780296 | tf_op jit(solution)/shard_map/ppermute | solution.py:10
  178.1 10.6 %copy-start.3 = (f32[256,1024]{1,0:T(8,128)S(1)}, f32[256,1024]{1,0:T(8,128)}, u32[]{:S(2)}) copy-start(f32[256,1024]{1,0:T(8,128)} %reduce-scatter.3.cloned.1.call-done) | copy-start | bytes 3145732
  178.1 10.6 %copy-start.6 = (bf16[256,1024]{1,0:T(8,128)(2,1)S(1)}, bf16[256,1024]{1,0:T(8,128)(2,1)}, u32[]{:S(2)}) copy-start(bf16[256,1024]{1,0:T(8,128)(2,1)} %param.6) | copy-start | bytes 1572868
  188.8 1.5 copy-start.2
  190.2 225.9 %all-reduce.2.cloned.1.call-start = ((), (), s32[]{:S(2)}) async-start(), calls=%async_computation.5 | async-start | bytes 1048576 | tf_op jit(solution)/shard_map/psum | solution.py:52
  203.7 404.1 %reduce-scatter.5.cloned.1.call-start = ((), (), s32[]{:S(2)}) async-start(), calls=%async_computation.6 | async-start | bytes 17039360 | tf_op jit(solution)/shard_map/reduce_scatter | solution.py:54
  237.6 180.5 %copy-start.4 = (bf16[256,4096]{1,0:T(8,128)(2,1)S(1)}, bf16[256,4096]{1,0:T(8,128)(2,1)}, u32[]{:S(2)}) copy-start(bf16[256,4096]{1,0:T(8,128)(2,1)} %all-gather.3.cloned.1.call-done) | copy-start | bytes 6291460
Sparse Core Ops, SparseCore 0:
  10.8 85.9 all-gather.4
  104.6 44.8 reduce-scatter.2
  190.4 37.4 all-gather.2
  231.8 184.2 all-reduce.1
  421.0 186.7 reduce-scatter.4
where the time goes:
time: 615 us; the launch traced here: 614 us
  waiting for transfers between devices  522 us (85%)
  matrix products  55.7 us (9%)
  between operations  14 us (2%)
  starting transfers between devices  10.2 us (2%)
  local copies, waits for them, and re-layouts  6.47 us (1%)
    reduce_scatter x1, waiting for transfers between devices, body(): lax.psum_scatter(lax.dot_general(columns, upstream, (((0,), (0,)), ((), (...  183 us
    psum x1, waiting for transfers between devices, body(): grad_filter = lax.psum(filter_local, 'seq')  178 us
    all_gather x1, waiting for transfers between devices, body(): weight_cols = lax.all_gather(out_weight, 'seq', axis=0, tiled=True)  88.8 us
    reduce_scatter x1, waiting for transfers between devices, body(): lax.psum_scatter(partial_terms, 'ch', scatter_dimension=1, tiled=True)  45 us
    conv_general_dilated x3, matrix products, depthwise(): lax.conv_general_dilated(signal[None], kernel[:, None, :], (1,), 'VALID',...  31.8 us
    all_gather x1, waiting for transfers between devices, body(): gated_full = lax.all_gather(gated, 'ch', axis=1, tiled=True)  23.9 us
  transfers between devices with their start and end apart: 7, of which 6 were waited for; matrix products, arithmetic and copies ran while one was open for 5% of the time, Pallas kernels for 0%

commit v1 on v0

--- a/solution.py
+++ b/solution.py
@@ -49,7 +49,8 @@
     grad_key = (grad_keyed * value_stream.astype(jnp.float32)).astype(jnp.bfloat16)
     grad_value = (grad_keyed * key_stream.astype(jnp.float32)).astype(jnp.bfloat16)
     filter_local = depthwise(front_pad, grad_response)[::-1].T
-    grad_filter = lax.psum(filter_local, "seq")
+    big = jax.lax.all_gather(filter_local, "seq")
+    grad_filter = jnp.sum(big, axis=0)
     columns = lax.slice_in_dim(gated_full, 0, lax.axis_size("seq") * out_weight.shape[0], axis=1)
     grad_weight = lax.psum_scatter(
         lax.dot_general(

time: 615 us -> 572 us (0.930)
  waiting for transfers between devices: 522 us -> 444 us
  local copies, waits for them, and re-layouts: 6.47 us -> 35.2 us
  other arithmetic: 5.54 us -> 12.2 us
    psum x1 -> x0, waiting for transfers between devices: 178 us -> none  [body(): grad_filter = lax.psum(filter_local, 'seq')]
    all_gather x0 -> x1, waiting for transfers between devices: none -> 128 us  [body(): big = jax.lax.all_gather(filter_local, 'seq')]
    unnamed x24 -> x25, local copies, waits for them, and re-layouts: 2.19 us -> 30.9 us
    reduce_scatter x1, waiting for transfers between devices: 183 us -> 156 us  [body(): lax.psum_scatter(lax.dot_general(columns, upstream, (((0,), (0,)), ((), (...]
    reduce_sum x0 -> x1, other arithmetic: none -> 6.7 us  [body(): grad_filter = jnp.sum(big, axis=0)]
  transfers between devices with their start and end apart: 7 -> 7, of which waited for: 6 -> 6; matrix products, arithmetic and copies ran while one was open for 5% -> 12% of each run, Pallas kernels for 0% -> 0%
where the time goes in v1:
time: 572 us
  waiting for transfers between devices  444 us (78%)
  matrix products  55.7 us (10%)
  local copies, waits for them, and re-layouts  35.2 us (6%)
  between operations  14 us (2%)
  other arithmetic  12.2 us (2%)
  starting transfers between devices  10.2 us (2%)
    reduce_scatter x1, waiting for transfers between devices, body(): lax.psum_scatter(lax.dot_general(columns, upstream, (((0,), (0,)), ((), (...  156 us
    all_gather x1, waiting for transfers between devices, body(): big = jax.lax.all_gather(filter_local, 'seq')  128 us
    all_gather x1, waiting for transfers between devices, body(): weight_cols = lax.all_gather(out_weight, 'seq', axis=0, tiled=True)  88.8 us
    reduce_scatter x1, waiting for transfers between devices, body(): lax.psum_scatter(partial_terms, 'ch', scatter_dimension=1, tiled=True)  45 us
    conv_general_dilated x3, matrix products, depthwise(): lax.conv_general_dilated(signal[None], kernel[:, None, :], (1,), 'VALID',...  31.8 us
    unnamed x25, local copies, waits for them, and re-layouts  30.9 us
    all_gather x1, waiting for transfers between devices, body(): gated_full = lax.all_gather(gated, 'ch', axis=1, tiled=True)  23.9 us
  transfers between devices with their start and end apart: 7, of which 6 were waited for; matrix products, arithmetic and copies ran while one was open for 12% of the time, Pallas kernels for 0%

profile of v1, /device:TPU:2, one launch (start us, length us, event | category | flops | bytes accessed | tf_op | source)
XLA Modules:
  0.0 571.7 jit_solution(7199725875416674534)
XLA Ops:
  7.2 0.7 all-gather.7.cloned.1.call-update
  8.0 88.8 %all-gather.7.cloned.1.call-done = bf16[4096,1024]{1,0:T(8,128)(2,1)} async-done(((bf16[64,1024]{1,0:T(8,128)(2,1)}), bf16[4096,1024]{1,0:T(8,128)(2,1)}) %all-gather.7.cloned.1.call-update) | async-done | bytes 8388624 | tf_op jit(solution)/shard_map/all_gather | solution.py:36
  96.8 7.7 %fusion.12 = f32[256,4096]{1,0:T(8,128)} fusion(bf16[256,1024]{1,0:T(8,128)(2,1)S(1)} %copy-done, bf16[4096,1024]{1,0:T(8,128)(2,1)} %all-gather.7.cloned.1.call-done), kind=kOutput, calls=%fused_computation.23 | convolution fusion | flops 2147483648 | bytes 13107200 | tf_op jit(solution)/shard_map/dot_general | solution.py:40
  104.5 45.0 %reduce-scatter.3.cloned.1.call-done = f32[256,1024]{1,0:T(8,128)} async-done(((f32[256,4096]{1,0:T(8,128)}), f32[256,1024]{1,0:T(8,128)}) %reduce-scatter.3.cloned.1.call-update) | async-done | bytes 1048592 | tf_op jit(solution)/shard_map/reduce_scatter | solution.py:43
  149.5 1.4 convert_multiply_fusion.3
  151.0 1.3 collective-permute-start.1
  152.3 0.4 copy.25
  152.7 2.2 collective-permute-done.1
  154.9 1.2 maximum_bitcast_fusion
  156.1 10.6 %fusion = f32[1,256,1024]{2,0,1:T(1,128)S(1)} fusion(f32[128,1,1024]{2,1,0:T(1,128)S(1)} %copy.25, f32[1,383,1024]{2,1,0:T(8,128)S(1)} %maximum_bitcast_fusion), kind=kOutput, calls=%fused_computation.2 | convolution fusion | flops 402653184 | bytes 3141632 | tf_op jit(solution)/shard_map/conv_general_dilated | solution.py:14
  166.7 1.5 fusion.7
  168.2 0.1 slice.8
  168.3 8.5 %collective-permute-start = (bf16[127,1024]{1,0:T(8,128)(2,1)S(1)}, bf16[127,1024]{1,0:T(8,128)(2,1)S(1)}, u32[]{:S(2)}, u32[]{:S(2)}) collective-permute-start(bf16[127,1024]{1,0:T(8,128)(2,1)S(1)} %slice.8), channel_id=1, source_target_pairs={{0,4},{4,8},{8,12},{12,16},{16,20},{20,24},{24,28},{28,32},{32,36}... | collective-permute-start | bytes 780296 | tf_op jit(solution)/shard_map/ppermute | solution.py:10
  176.8 0.7 rev.6
  177.6 0.4 copy.23
  178.0 0.1 maximum_bitcast_fusion.1
  178.2 10.6 %fusion.4 = f32[1,256,1024]{2,0,1:T(1,128)S(1)} fusion(f32[128,1,1024]{2,1,0:T(1,128)S(1)} %copy.23, bf16[1,383,1024]{2,1,0:T(8,128)(2,1)S(1)} %maximum_bitcast_fusion.1), kind=kOutput, calls=%fused_computation.12 | convolution fusion | flops 402653184 | bytes 2357248 | tf_op jit(solution)/shard_map/conv_general_dilated | solution.py:14
  188.8 1.4 fusion.10
  190.2 0.0 all-gather.9.cloned.1.call-start
  190.3 10.7 %fusion.2 = f32[1,128,1024]{2,0,1:T(1,128)S(1)} fusion(bf16[1,383,1024]{2,1,0:T(8,128)(2,1)S(1)} %maximum_bitcast_fusion.1, f32[256,1,1024]{2,0,1:T(8,128)S(1)} %bitcast.35), kind=kOutput, calls=%fused_computation.10 | convolution fusion | flops 402653184 | bytes 2357248 | tf_op jit(solution)/shard_map/conv_general_dilated | solution.py:14
  201.0 0.1 copy.46
  201.1 2.7 rev.7
  203.7 0.2 reduce-scatter.5.cloned.1.call-start
  204.0 23.9 %all-gather.5.cloned.1.call-done = bf16[256,4096]{1,0:T(8,128)(2,1)} async-done(((bf16[256,1024]{1,0:T(8,128)(2,1)}), bf16[256,4096]{1,0:T(8,128)(2,1)}) %all-gather.5.cloned.1.call-update) | async-done | bytes 2097168 | tf_op jit(solution)/shard_map/all_gather | solution.py:35
  227.9 9.7 %fusion.13 = f32[4096,1024]{1,0:T(8,128)} fusion(bf16[256,4096]{1,0:T(8,128)(2,1)} %all-gather.5.cloned.1.call-done, bf16[256,1024]{1,0:T(8,128)(2,1)S(1)} %copy-done), kind=kOutput, calls=%fused_computation.24 | convolution fusion | flops 2147483648 | bytes 19398656 | tf_op jit(solution)/shard_map/dot_general | solution.py:56
  237.6 1.6 copy-done.4
  239.2 6.5 %convolution_convert_fusion = bf16[256,1024]{1,0:T(8,128)(2,1)} fusion(bf16[256,4096]{1,0:T(8,128)(2,1)S(1)} %copy-done.4, bf16[4096,1024]{1,0:T(8,128)(2,1)} %all-gather.7.cloned.1.call-done), kind=kOutput, calls=%fused_computation.9 | convolution fusion | flops 2147745792 | bytes 11010048 | tf_op jit(solution)/shard_map/dot_general | solution.py:37
  245.7 127.8 %all-gather.9.cloned.1.call-done = f32[65536,128]{0,1:T(8,128)} async-done(((f32[1024,128]{0,1:T(8,128)}), f32[65536,128]{0,1:T(8,128)}) %all-gather.9.cloned.1.call-update) | async-done | bytes 33554448 | tf_op jit(solution)/shard_map/all_gather | solution.py:52
  373.4 28.2 %copy.32 = f32[16,8,64,1024]{3,2,1,0:T(8,128)S(1)} copy(f32[16,8,64,1024]{3,1,2,0:T(8,128)} %bitcast.34) | data formatting | bytes 67108864
  401.6 6.7 %bitcast_reduce_fusion = f32[1024,128]{0,1:T(8,128)S(1)} fusion(f32[16,8,64,1024]{3,2,1,0:T(8,128)S(1)} %copy.32), kind=kLoop, calls=%fused_computation | loop fusion | flops 8257536 | bytes 34078720 | tf_op jit(solution)/shard_map/reduce_sum | solution.py:53
  408.4 1.0 copy.28
  409.4 155.8 %reduce-scatter.5.cloned.1.call-done = f32[64,1024]{1,0:T(8,128)} async-done(((f32[4096,1024]{1,0:T(8,128)}), f32[64,1024]{1,0:T(8,128)}) %reduce-scatter.5.cloned.1.call-update) | async-done | bytes 262160 | tf_op jit(solution)/shard_map/reduce_scatter | solution.py:55
  (30 shorter events, 0.3 us)
Async XLA Ops:
  7.2 89.6 %copy-start = (bf16[256,1024]{1,0:T(8,128)(2,1)S(1)}, bf16[256,1024]{1,0:T(8,128)(2,1)}, u32[]{:S(2)}) copy-start(bf16[256,1024]{1,0:T(8,128)(2,1)} %param.11) | copy-start | bytes 1572868
  7.2 89.6 %all-gather.7.cloned.1.call-start = ((), (), s32[]{:S(2)}) async-start(), calls=%async_computation.3 | async-start | bytes 8519680 | tf_op jit(solution)/shard_map/all_gather | solution.py:36
  7.9 141.6 %reduce-scatter.3.cloned.1.call-start = ((), (), s32[]{:S(2)}) async-start(), calls=%async_computation.4 | async-start | bytes 5242880 | tf_op jit(solution)/shard_map/reduce_scatter | solution.py:43
  104.4 45.1 %copy-start.5 = (bf16[256,1024]{1,0:T(8,128)(2,1)S(1)}, bf16[256,1024]{1,0:T(8,128)(2,1)}, u32[]{:S(2)}) copy-start(bf16[256,1024]{1,0:T(8,128)(2,1)} %param.6) | copy-start | bytes 1572868
  104.5 47.8 %copy-start.7 = (f32[1024,128]{1,0:T(8,128)S(1)}, f32[1024,128]{1,0:T(8,128)}, u32[]{:S(2)}) copy-start(f32[1024,128]{1,0:T(8,128)} %param.9) | copy-start | bytes 1572868
  104.5 123.4 %all-gather.5.cloned.1.call-start = ((), (), s32[]{:S(2)}) async-start(), calls=%async_computation.2 | async-start | bytes 2621440 | tf_op jit(solution)/shard_map/all_gather | solution.py:35
  150.9 5.2 copy-start.1
  151.0 3.9 collective-permute-start.1
  156.1 10.6 %copy-start.9 = (bf16[256,1024]{1,0:T(8,128)(2,1)S(1)}, bf16[256,1024]{1,0:T(8,128)(2,1)}, u32[]{:S(2)}) copy-start(bf16[256,1024]{1,0:T(8,128)(2,1)} %param.7) | copy-start | bytes 1572868
  156.1 10.6 %copy-start.10 = (bf16[256,1024]{1,0:T(8,128)(2,1)S(1)}, bf16[256,1024]{1,0:T(8,128)(2,1)}, u32[]{:S(2)}) copy-start(bf16[256,1024]{1,0:T(8,128)(2,1)} %param.8) | copy-start | bytes 1572868
  166.7 10.1 %copy-start.8 = (f32[1024,128]{1,0:T(8,128)S(1)}, f32[1024,128]{1,0:T(8,128)}, u32[]{:S(2)}) copy-start(f32[1024,128]{1,0:T(8,128)} %param.9) | copy-start | bytes 1572868
  168.3 9.7 %collective-permute-start = (bf16[127,1024]{1,0:T(8,128)(2,1)S(1)}, bf16[127,1024]{1,0:T(8,128)(2,1)S(1)}, u32[]{:S(2)}, u32[]{:S(2)}) collective-permute-start(bf16[127,1024]{1,0:T(8,128)(2,1)S(1)} %slice.8), channel_id=1, source_target_pairs={{0,4},{4,8},{8,12},{12,16},{16,20},{20,24},{24,28},{28,32},{32,36}... | collective-permute-start | bytes 780296 | tf_op jit(solution)/shard_map/ppermute | solution.py:10
  178.1 10.6 %copy-start.3 = (f32[256,1024]{1,0:T(8,128)S(1)}, f32[256,1024]{1,0:T(8,128)}, u32[]{:S(2)}) copy-start(f32[256,1024]{1,0:T(8,128)} %reduce-scatter.3.cloned.1.call-done) | copy-start | bytes 3145732
  178.1 10.6 %copy-start.6 = (bf16[256,1024]{1,0:T(8,128)(2,1)S(1)}, bf16[256,1024]{1,0:T(8,128)(2,1)}, u32[]{:S(2)}) copy-start(bf16[256,1024]{1,0:T(8,128)(2,1)} %param.6) | copy-start | bytes 1572868
  188.8 1.5 copy-start.2
  190.2 183.2 %all-gather.9.cloned.1.call-start = ((), (), s32[]{:S(2)}) async-start(), calls=%async_computation.6 | async-start | bytes 34078720 | tf_op jit(solution)/shard_map/all_gather | solution.py:52
  203.7 361.4 %reduce-scatter.5.cloned.1.call-start = ((), (), s32[]{:S(2)}) async-start(), calls=%async_computation.5 | async-start | bytes 17039360 | tf_op jit(solution)/shard_map/reduce_scatter | solution.py:55
  237.6 1.6 copy-start.4
Sparse Core Ops, SparseCore 0:
  10.8 85.9 all-gather.6
  104.6 44.8 reduce-scatter.2
  190.4 37.4 all-gather.4
  230.5 142.8 all-gather.8
  378.3 186.7 reduce-scatter.4
